TPU v7x, 32 devices: a whole 2x2x4 slice. The times are simulated.
32 devices in a mesh: row: 4 (over y, x), col: 8 (over z, core).
Axes of the slice: x: 2, y: 2, z: 4, core: 2. Of those that a mesh axis runs over, the one named last changes fastest.
Arguments:
- frames: bfloat16 [4096, 440], P('col'), may hold values from -6 to 6
- center_picks: int32 [8, 8, 64], P('col'), may hold values from 0 to 511, as said below
- send_counts: int32 [8, 8], P(None, 'col'), may hold values from 0 to 64, as said below
- send_offsets: int32 [8, 8], P(None, 'col'), may hold values from 0 to 256, as said below
Outputs:
- factor_panels: float32 [4, 512, 1024], P('row', 'col')
- trailing: float32 [4, 512, 8, 256], P('row', None, 'col')
Inputs may be any that keep to these rules, and one draw needn't show every extreme that they name: `center_picks`: for each owner the entries over all destinations and slots are distinct local frame indices. `send_counts`: for each destination the counts over owners sum to 256; every destination has an owner that fills all 64 slots and one that sends nothing. `send_offsets`: for each destination the owners' segments [offset, offset + count) cover 0 to 255 without intersection, in an order that varies by destination; an owner that sends nothing may start at 256.
All inputs are finite; a program needn't handle non-finite values.
Results may differ from a plain program's by a relative error of at most 0.0003.
Values may be sent and summed in bfloat16 or wider, within the bound.
No kernel may reach another device: no remote copies, remote signals or barrier semaphores. Data moves between devices by JAX's collectives and lax.ppermute only.
A program may use at most 128 MiB of HBM per device.

v0:
```python
import jax
import jax.numpy as jnp
from jax import lax
from jax.sharding import PartitionSpec as P

PANEL = 256
PANELS = 4
CENT_DEV = 256
kernel_scale = 0.6
ridge_shift = 0.1


def spread(value, axis, source):
    kept = jnp.where(lax.axis_index(axis) == source, value, 0).astype(value.dtype)
    return lax.psum(kept, axis)


def gaussian(left_feats, right_feats):
    inner = lax.dot_general(
        left_feats, right_feats, (((1,), (1,)), ((), ())), preferred_element_type=jnp.float32
    )
    left_norm = jnp.sum(jnp.square(left_feats.astype(jnp.float32)), axis=1)
    right_norm = jnp.sum(jnp.square(right_feats.astype(jnp.float32)), axis=1)
    feat_width = left_feats.shape[1]
    return jnp.exp(
        -(kernel_scale / feat_width) * (left_norm[:, None] + right_norm[None, :] - 2.0 * inner)
    )


def outer_minus(column, panel_cols, rows_piece):
    return column - lax.dot_general(
        panel_cols,
        rows_piece,
        (((1,), (1,)), ((), ())),
        precision=lax.Precision.HIGHEST,
        preferred_element_type=jnp.float32,
    )


def make_panel(column, factor, row_tile, panel_step):
    solved = jax.scipy.linalg.solve_triangular(factor, column.T, lower=True).T
    repeated = jnp.tile(factor, (column.shape[0] // factor.shape[0], 1))
    return jnp.where(
        (row_tile > panel_step)[:, None],
        solved,
        jnp.where((row_tile == panel_step)[:, None], repeated, jnp.zeros_like(solved)),
    )


def update_slots(columns, panel_cols, col_rows):
    columns[0] = outer_minus(columns[0], panel_cols, col_rows)
    return columns


def per_device(frames, center_picks, send_counts, send_offsets):
    rows_axis = lax.axis_size("row")
    cols_axis = lax.axis_size("col")
    row_id = lax.axis_index("row")
    col_id = lax.axis_index("col")
    feat_width = frames.shape[1]
    capacity = center_picks.shape[2]
    outgoing = frames[center_picks[0]]
    incoming = lax.all_to_all(outgoing, "col", split_axis=0, concat_axis=0, tiled=True)
    position = jnp.arange(CENT_DEV, dtype=jnp.int32)
    starts = send_offsets[:, 0]
    lengths = send_counts[:, 0]
    inside = (position[:, None] >= starts[None, :]) & (
        position[:, None] < (starts + lengths)[None, :]
    )
    source = jnp.sum(jnp.where(inside, jnp.arange(cols_axis, dtype=jnp.int32)[None, :], 0), axis=1)
    within = position - jnp.sum(jnp.where(inside, starts[None, :], 0), axis=1)
    own_feats = incoming.reshape(cols_axis * capacity, feat_width)[source * capacity + within]
    col_slots = CENT_DEV // PANEL
    row_tiles_dev = col_slots * cols_axis // rows_axis
    rows_dev = row_tiles_dev * PANEL
    tile_range = jnp.arange(row_tiles_dev, dtype=jnp.int32)
    gathered = lax.all_gather(own_feats, "col", axis=0, tiled=True)
    blocks = gathered.reshape(cols_axis, col_slots, PANEL, feat_width)
    my_tiles = row_id + rows_axis * tile_range
    row_feats = blocks[my_tiles % cols_axis, my_tiles // cols_axis].reshape(rows_dev, feat_width)
    local_rows = jnp.arange(rows_dev, dtype=jnp.int32)
    row_tile = row_id + rows_axis * (local_rows // PANEL)
    global_row = row_tile * PANEL + local_rows % PANEL
    local_cols = jnp.arange(CENT_DEV, dtype=jnp.int32)
    global_col = (col_id + cols_axis * (local_cols // PANEL)) * PANEL + local_cols % PANEL
    kernel = gaussian(row_feats, own_feats) + ridge_shift * (
        global_row[:, None] == global_col[None, :]
    ).astype(jnp.float32)
    columns = [kernel]
    panels = []
    for panel_step in range(PANELS):
        slot_now = panel_step // cols_axis
        tile_slot = panel_step // rows_axis
        diag_here = columns[slot_now][tile_slot * PANEL : (tile_slot + 1) * PANEL]
        diag_block = spread(diag_here, "row", panel_step % rows_axis)
        factor = jnp.linalg.cholesky(diag_block)
        panel_here = make_panel(columns[slot_now], factor, row_tile, panel_step)
        panel_cols = spread(panel_here, "col", panel_step % cols_axis)
        here_rows = lax.dynamic_slice_in_dim(
            panel_cols, (col_id + 0) // rows_axis * PANEL, PANEL, 0
        )
        col_rows = spread(here_rows, "row", col_id % rows_axis)
        panels.append(panel_cols)
        columns = update_slots(columns, panel_cols, col_rows)
    trailing = columns[0].reshape(1, rows_dev, 1, CENT_DEV)
    every_panel = jnp.concatenate(panels, axis=1)
    share_rows = rows_dev // cols_axis
    panel_share = lax.dynamic_slice_in_dim(every_panel, col_id * share_rows, share_rows, 0).reshape(
        1, share_rows, PANELS * PANEL
    )
    return (panel_share, trailing)


def solution(mesh):
    in_specs = (P("col", None), P("col", None, None), P(None, "col"), P(None, "col"))
    out_specs = (P("row", "col", None), P("row", None, "col", None))
    return jax.shard_map(
        per_device, mesh=mesh, in_specs=in_specs, out_specs=out_specs, check_vma=False
    )
```

profile of v0, /device:TPU:0, one launch (start us, length us, event | category | flops | bytes accessed | tf_op | source)
XLA Modules:
  0.0 926.6 jit_solution(15417714206202597751)
XLA Ops:
  9.2 2.6 gather_fusion
  11.8 6.3 all-to-all-start
  18.3 15.2 %all-to-all-done = bf16[8,64,440]{2,1,0:T(8,128)(2,1)S(1)} async-done(((bf16[8,64,440]{2,1,0:T(8,128)(2,1)}), bf16[8,64,440]{2,1,0:T(8,128)(2,1)S(1)}, u32[]{:S(2)}, u32[]{:S(2)}) %all-to-all-start) | async-done | bytes 450592 | tf_op jit(solution)/shard_map/all_to_all | solution.py:63
  33.5 1.9 gather_fusion.1
  36.6 27.0 %all-gather.3.cloned.1.call-done = bf16[2048,440]{1,0:T(8,128)(2,1)} async-done(((bf16[256,440]{1,0:T(8,128)(2,1)}), bf16[2048,440]{1,0:T(8,128)(2,1)}) %all-gather.3.cloned.1.call-update) | async-done | bytes 1802256 | tf_op jit(solution)/shard_map/all_gather | solution.py:77
  63.5 2.2 gather_fusion.2
  67.6 42.3 %all-reduce.14.cloned.1.call-done = f32[256,256]{0,1:T(8,128)} async-done(((f32[256,256]{0,1:T(8,128)}), f32[256,256]{0,1:T(8,128)}) %all-reduce.14.cloned.1.call-update) | async-done | bytes 262160 | tf_op jit(solution)/shard_map/psum | solution.py:15
  112.0 11.7 %cholesky.214 = f32[128,128]{1,0:T(8,128)S(1)} custom-call(f32[128,128]{1,0:T(8,128)S(1)} %cholesky.346), custom_call_target="Cholesky" | custom-call | tf_op jit(solution)/shard_map/jit(cholesky)/cholesky | solution.py:96
  123.7 9.8 %custom-call.19 = f32[1,128,128]{1,2,0:T(8,128)S(1)} custom-call(f32[1,128,128]{2,1,0:T(8,128)S(1)} %get-tuple-element.105), custom_call_target="InvertDiagBlocksLowerTriangular" | custom-call | tf_op jit(solution)/shard_map/jit(cholesky)/cholesky | solution.py:96
  134.0 11.7 %cholesky.231 = f32[128,128]{1,0:T(8,128)S(1)} custom-call(f32[128,128]{1,0:T(8,128)S(1)} %convolution_subtract_fusion.8), custom_call_target="Cholesky" | custom-call | tf_op jit(solution)/shard_map/jit(cholesky)/cholesky | solution.py:96
  148.0 4.6 while.8
  152.6 19.7 %custom-call.20 = f32[2,128,128]{1,2,0:T(8,128)S(1)} custom-call(f32[2,128,128]{2,1,0:T(8,128)S(1)} %get-tuple-element.30), custom_call_target="InvertDiagBlocksLowerTriangular" | custom-call | tf_op jit(solution)/shard_map/jit(_solve_triangular)/triangular_solve | solution.py:41
  174.8 56.2 %all-reduce.16.cloned.1.call-done = f32[512,256]{0,1:T(8,128)} async-done(((f32[512,256]{0,1:T(8,128)}), f32[512,256]{0,1:T(8,128)}) %all-reduce.16.cloned.1.call-update) | async-done | bytes 524304 | tf_op jit(solution)/shard_map/psum | solution.py:15
  231.1 1.7 dynamic-slice_select_fusion.3
  232.8 43.5 %all-reduce.18.cloned.1.call-done = f32[256,256]{0,1:T(8,128)} async-done(((f32[256,256]{0,1:T(8,128)}), f32[256,256]{0,1:T(8,128)}) %all-reduce.18.cloned.1.call-update) | async-done | bytes 262160 | tf_op jit(solution)/shard_map/psum | solution.py:15
  276.4 1.8 bitcast_subtract_fusion.2
  279.2 43.7 %all-reduce.20.cloned.1.call-done = f32[256,256]{0,1:T(8,128)} async-done(((f32[256,256]{0,1:T(8,128)}), f32[256,256]{0,1:T(8,128)}) %all-reduce.20.cloned.1.call-update) | async-done | bytes 262160 | tf_op jit(solution)/shard_map/psum | solution.py:15
  325.0 11.7 %cholesky.248 = f32[128,128]{1,0:T(8,128)S(1)} custom-call(f32[128,128]{1,0:T(8,128)S(1)} %cholesky.349), custom_call_target="Cholesky" | custom-call | tf_op jit(solution)/shard_map/jit(cholesky)/cholesky | solution.py:96
  336.8 9.8 %custom-call.21 = f32[1,128,128]{1,2,0:T(8,128)S(1)} custom-call(f32[1,128,128]{2,1,0:T(8,128)S(1)} %get-tuple-element.101), custom_call_target="InvertDiagBlocksLowerTriangular" | custom-call | tf_op jit(solution)/shard_map/jit(cholesky)/cholesky | solution.py:96
  347.1 11.7 %cholesky.265 = f32[128,128]{1,0:T(8,128)S(1)} custom-call(f32[128,128]{1,0:T(8,128)S(1)} %convolution_subtract_fusion.7), custom_call_target="Cholesky" | custom-call | tf_op jit(solution)/shard_map/jit(cholesky)/cholesky | solution.py:96
  361.6 4.3 while.9
  365.9 19.7 %custom-call.22 = f32[2,128,128]{1,2,0:T(8,128)S(1)} custom-call(f32[2,128,128]{2,1,0:T(8,128)S(1)} %get-tuple-element.31), custom_call_target="InvertDiagBlocksLowerTriangular" | custom-call | tf_op jit(solution)/shard_map/jit(_solve_triangular)/triangular_solve | solution.py:41
  388.1 56.3 %all-reduce.22.cloned.1.call-done = f32[512,256]{0,1:T(8,128)} async-done(((f32[512,256]{0,1:T(8,128)}), f32[512,256]{0,1:T(8,128)}) %all-reduce.22.cloned.1.call-update) | async-done | bytes 524304 | tf_op jit(solution)/shard_map/psum | solution.py:15
  444.4 1.7 dynamic-slice_select_fusion.2
  446.2 43.9 %all-reduce.24.cloned.1.call-done = f32[256,256]{0,1:T(8,128)} async-done(((f32[256,256]{0,1:T(8,128)}), f32[256,256]{0,1:T(8,128)}) %all-reduce.24.cloned.1.call-update) | async-done | bytes 262160 | tf_op jit(solution)/shard_map/psum | solution.py:15
  490.1 1.8 bitcast_subtract_fusion.1
  492.8 43.8 %all-reduce.26.cloned.1.call-done = f32[256,256]{0,1:T(8,128)} async-done(((f32[256,256]{0,1:T(8,128)}), f32[256,256]{0,1:T(8,128)}) %all-reduce.26.cloned.1.call-update) | async-done | bytes 262160 | tf_op jit(solution)/shard_map/psum | solution.py:15
  538.6 11.7 %cholesky.282 = f32[128,128]{1,0:T(8,128)S(1)} custom-call(f32[128,128]{1,0:T(8,128)S(1)} %cholesky.352), custom_call_target="Cholesky" | custom-call | tf_op jit(solution)/shard_map/jit(cholesky)/cholesky | solution.py:96
  550.4 9.8 %custom-call.23 = f32[1,128,128]{1,2,0:T(8,128)S(1)} custom-call(f32[1,128,128]{2,1,0:T(8,128)S(1)} %get-tuple-element.97), custom_call_target="InvertDiagBlocksLowerTriangular" | custom-call | tf_op jit(solution)/shard_map/jit(cholesky)/cholesky | solution.py:96
  560.7 11.7 %cholesky.299 = f32[128,128]{1,0:T(8,128)S(1)} custom-call(f32[128,128]{1,0:T(8,128)S(1)} %convolution_subtract_fusion.6), custom_call_target="Cholesky" | custom-call | tf_op jit(solution)/shard_map/jit(cholesky)/cholesky | solution.py:96
  575.2 4.3 while.10
  576.0 1.4 bitcast_dynamic-update-slice_fusion.10
  578.1 1.4 bitcast_dynamic-update-slice_fusion.10
  579.5 19.7 %custom-call.24 = f32[2,128,128]{1,2,0:T(8,128)S(1)} custom-call(f32[2,128,128]{2,1,0:T(8,128)S(1)} %get-tuple-element.32), custom_call_target="InvertDiagBlocksLowerTriangular" | custom-call | tf_op jit(solution)/shard_map/jit(_solve_triangular)/triangular_solve | solution.py:41
  601.8 56.3 %all-reduce.28.cloned.1.call-done = f32[512,256]{0,1:T(8,128)} async-done(((f32[512,256]{0,1:T(8,128)}), f32[512,256]{0,1:T(8,128)}) %all-reduce.28.cloned.1.call-update) | async-done | bytes 524304 | tf_op jit(solution)/shard_map/psum | solution.py:15
  658.1 1.7 dynamic-slice_select_fusion.1
  659.8 43.5 %all-reduce.30.cloned.1.call-done = f32[256,256]{0,1:T(8,128)} async-done(((f32[256,256]{0,1:T(8,128)}), f32[256,256]{0,1:T(8,128)}) %all-reduce.30.cloned.1.call-update) | async-done | bytes 262160 | tf_op jit(solution)/shard_map/psum | solution.py:15
  703.3 1.8 bitcast_subtract_fusion
  706.0 44.0 %all-reduce.32.cloned.1.call-done = f32[256,256]{0,1:T(8,128)} async-done(((f32[256,256]{0,1:T(8,128)}), f32[256,256]{0,1:T(8,128)}) %all-reduce.32.cloned.1.call-update) | async-done | bytes 262160 | tf_op jit(solution)/shard_map/psum | solution.py:15
  752.1 11.7 %cholesky.316 = f32[128,128]{1,0:T(8,128)S(1)} custom-call(f32[128,128]{1,0:T(8,128)S(1)} %cholesky.355), custom_call_target="Cholesky" | custom-call | tf_op jit(solution)/shard_map/jit(cholesky)/cholesky | solution.py:96
  763.9 9.8 %custom-call.25 = f32[1,128,128]{1,2,0:T(8,128)S(1)} custom-call(f32[1,128,128]{2,1,0:T(8,128)S(1)} %get-tuple-element.93), custom_call_target="InvertDiagBlocksLowerTriangular" | custom-call | tf_op jit(solution)/shard_map/jit(cholesky)/cholesky | solution.py:96
  774.2 11.7 %cholesky.333 = f32[128,128]{1,0:T(8,128)S(1)} custom-call(f32[128,128]{1,0:T(8,128)S(1)} %convolution_subtract_fusion.5), custom_call_target="Cholesky" | custom-call | tf_op jit(solution)/shard_map/jit(cholesky)/cholesky | solution.py:96
  788.6 4.2 while.11
  792.8 19.7 %custom-call.26 = f32[2,128,128]{1,2,0:T(8,128)S(1)} custom-call(f32[2,128,128]{2,1,0:T(8,128)S(1)} %get-tuple-element.33), custom_call_target="InvertDiagBlocksLowerTriangular" | custom-call | tf_op jit(solution)/shard_map/jit(_solve_triangular)/triangular_solve | solution.py:41
  815.1 56.3 %all-reduce.34.cloned.1.call-done = f32[512,256]{0,1:T(8,128)} async-done(((f32[512,256]{0,1:T(8,128)}), f32[512,256]{0,1:T(8,128)}) %all-reduce.34.cloned.1.call-update) | async-done | bytes 524304 | tf_op jit(solution)/shard_map/psum | solution.py:15
  871.3 1.7 dynamic-slice_select_fusion
  875.1 41.9 %all-reduce.36.cloned.1.call-done = f32[256,256]{0,1:T(8,128)} async-done(((f32[256,256]{0,1:T(8,128)}), f32[256,256]{0,1:T(8,128)}) %all-reduce.36.cloned.1.call-update) | async-done | bytes 262160 | tf_op jit(solution)/shard_map/psum | solution.py:15
  917.0 1.6 fusion
  (170 shorter events, 49.9 us)
Async XLA Ops:
  9.2 9.0 copy-start.5
  9.2 9.0 copy-start.6
  11.8 21.7 %all-to-all-start = ((bf16[8,64,440]{2,1,0:T(8,128)(2,1)}), bf16[8,64,440]{2,1,0:T(8,128)(2,1)S(1)}, u32[]{:S(2)}, u32[]{:S(2)}) async-start(bf16[8,64,440]{2,1,0:T(8,128)(2,1)} %bitcast.1), calls=%async_computation | async-start | bytes 1048576 | tf_op jit(solution)/shard_map/all_to_all | solution.py:63
  18.1 45.4 %all-gather.3.cloned.1.call-start = ((), (), s32[]{:S(2)}) async-start(), calls=%async_computation.13 | async-start | bytes 2359296 | tf_op jit(solution)/shard_map/all_gather | solution.py:77
  35.3 30.6 %copy-start.4 = (bf16[256,440]{1,0:T(8,128)(2,1)S(1)}, bf16[256,440]{1,0:T(8,128)(2,1)}, u32[]{:S(2)}) copy-start(bf16[256,440]{1,0:T(8,128)(2,1)} %gather_fusion.1) | copy-start | bytes 675844
  35.4 74.5 %all-reduce.14.cloned.1.call-start = ((), (), s32[]{:S(2)}) async-start(), calls=%async_computation.1 | async-start | bytes 524288 | tf_op jit(solution)/shard_map/psum | solution.py:15
  67.3 163.8 %all-reduce.16.cloned.1.call-start = ((), (), s32[]{:S(2)}) async-start(), calls=%async_computation.2 | async-start | bytes 1048576 | tf_op jit(solution)/shard_map/psum | solution.py:15
  174.8 101.6 %all-reduce.18.cloned.1.call-start = ((), (), s32[]{:S(2)}) async-start(), calls=%async_computation.3 | async-start | bytes 524288 | tf_op jit(solution)/shard_map/psum | solution.py:15
  232.8 90.2 %all-reduce.20.cloned.1.call-start = ((), (), s32[]{:S(2)}) async-start(), calls=%async_computation.4 | async-start | bytes 524288 | tf_op jit(solution)/shard_map/psum | solution.py:15
  279.1 165.3 %all-reduce.22.cloned.1.call-start = ((), (), s32[]{:S(2)}) async-start(), calls=%async_computation.5 | async-start | bytes 1048576 | tf_op jit(solution)/shard_map/psum | solution.py:15
  388.1 102.0 %all-reduce.24.cloned.1.call-start = ((), (), s32[]{:S(2)}) async-start(), calls=%async_computation.6 | async-start | bytes 524288 | tf_op jit(solution)/shard_map/psum | solution.py:15
  446.1 90.5 %all-reduce.26.cloned.1.call-start = ((), (), s32[]{:S(2)}) async-start(), calls=%async_computation.7 | async-start | bytes 524288 | tf_op jit(solution)/shard_map/psum | solution.py:15
  492.7 165.4 %all-reduce.28.cloned.1.call-start = ((), (), s32[]{:S(2)}) async-start(), calls=%async_computation.8 | async-start | bytes 1048576 | tf_op jit(solution)/shard_map/psum | solution.py:15
  601.7 101.6 %all-reduce.30.cloned.1.call-start = ((), (), s32[]{:S(2)}) async-start(), calls=%async_computation.9 | async-start | bytes 524288 | tf_op jit(solution)/shard_map/psum | solution.py:15
  659.8 90.3 %all-reduce.32.cloned.1.call-start = ((), (), s32[]{:S(2)}) async-start(), calls=%async_computation.10 | async-start | bytes 524288 | tf_op jit(solution)/shard_map/psum | solution.py:15
  706.0 165.4 %all-reduce.34.cloned.1.call-start = ((), (), s32[]{:S(2)}) async-start(), calls=%async_computation.11 | async-start | bytes 1048576 | tf_op jit(solution)/shard_map/psum | solution.py:15
  814.0 59.1 %copy-start.1 = (f32[512,256]{0,1:T(8,128)S(1)}, f32[512,256]{0,1:T(8,128)}, u32[]{:S(2)}) copy-start(f32[512,256]{0,1:T(8,128)} %all-reduce.16.cloned.1.call-done) | copy-start | bytes 1572868
  814.0 59.1 %copy-start.2 = (f32[512,256]{0,1:T(8,128)S(1)}, f32[512,256]{0,1:T(8,128)}, u32[]{:S(2)}) copy-start(f32[512,256]{0,1:T(8,128)} %all-reduce.22.cloned.1.call-done) | copy-start | bytes 1572868
  814.0 59.1 %copy-start.3 = (f32[512,256]{0,1:T(8,128)S(1)}, f32[512,256]{0,1:T(8,128)}, u32[]{:S(2)}) copy-start(f32[512,256]{0,1:T(8,128)} %all-reduce.28.cloned.1.call-done) | copy-start | bytes 1572868
  815.0 102.0 %all-reduce.36.cloned.1.call-start = ((), (), s32[]{:S(2)}) async-start(), calls=%async_computation.12 | async-start | bytes 524288 | tf_op jit(solution)/shard_map/psum | solution.py:15
  871.3 45.7 %copy-start = (f32[512,256]{0,1:T(8,128)S(1)}, f32[512,256]{0,1:T(8,128)}, u32[]{:S(2)}) copy-start(f32[512,256]{0,1:T(8,128)} %all-reduce.34.cloned.1.call-done) | copy-start | bytes 1572868
Sparse Core Ops, SparseCore 0:
  35.5 27.9 all-gather.2
  67.4 42.4 all-reduce.13
  174.9 56.1 all-reduce.15
  234.4 41.8 all-reduce.17
  280.0 42.9 all-reduce.19
  388.2 56.1 all-reduce.21
  448.2 41.8 all-reduce.23
  493.6 42.9 all-reduce.25
  601.9 56.1 all-reduce.27
  661.4 41.9 all-reduce.29
  707.1 42.9 all-reduce.31
  815.1 56.1 all-reduce.33
  875.1 41.8 all-reduce.35
where the time goes:
time: 930 us; the launch traced here: 927 us
  waiting for transfers between devices  614 us (66%)
  other arithmetic  238 us (26%)
  local copies, waits for them, and re-layouts  31.9 us (3%)
  between operations  20.4 us (2%)
  matrix products  14 us (2%)
    psum x12, waiting for transfers between devices, spread(): return lax.psum(kept, axis)  572 us
    another operation x27, other arithmetic, per_device(): factor = jnp.linalg.cholesky(diag_block)  138 us
    another operation x9, other arithmetic, make_panel(): solved = jax.scipy.linalg.solve_triangular(factor, column.T, lower=True).T  78.8 us
    all_gather x1, waiting for transfers between devices, per_device(): gathered = lax.all_gather(own_feats, 'col', axis=0, tiled=True)  27 us
  transfers between devices with their start and end apart: 14, of which 14 were waited for; matrix products, arithmetic and copies ran while one was open for 0% of the time, Pallas kernels for 0%

commit v1 on v0

--- a/solution.py
+++ b/solution.py
@@ -8,6 +8,18 @@
 CENT_DEV = 256
 kernel_scale = 0.6
 ridge_shift = 0.1
+
+
+def doubled_up(x, axis, dim):
+    ways, here = (lax.axis_size(axis), lax.axis_index(axis))
+    grown, reach = (x, 1)
+    while reach < ways:
+        theirs = lax.ppermute(grown, axis, [(d, d ^ reach) for d in range(ways)])
+        mine_first = jnp.concatenate([grown, theirs], axis=dim)
+        theirs_first = jnp.concatenate([theirs, grown], axis=dim)
+        grown = jnp.where(here & reach == 0, mine_first, theirs_first)
+        reach = 2 * reach
+    return grown
 
 
 def spread(value, axis, source):
@@ -74,7 +86,7 @@
     row_tiles_dev = col_slots * cols_axis // rows_axis
     rows_dev = row_tiles_dev * PANEL
     tile_range = jnp.arange(row_tiles_dev, dtype=jnp.int32)
-    gathered = lax.all_gather(own_feats, "col", axis=0, tiled=True)
+    gathered = doubled_up(own_feats, "col", 0)
     blocks = gathered.reshape(cols_axis, col_slots, PANEL, feat_width)
     my_tiles = row_id + rows_axis * tile_range
     row_feats = blocks[my_tiles % cols_axis, my_tiles // cols_axis].reshape(rows_dev, feat_width)

time: 930 us -> 964 us (1.037)
  waiting for transfers between devices: 614 us -> 643 us
    ppermute x0 -> x3, waiting for transfers between devices: none -> 56.6 us  [doubled_up(): theirs = lax.ppermute(grown, axis, [(d, d ^ reach) for d in range(ways)])]
    all_gather x1 -> x0, waiting for transfers between devices: 27 us -> none  [per_device(): gathered = lax.all_gather(own_feats, 'col', axis=0, tiled=True)]
  transfers between devices with their start and end apart: 14 -> 16, of which waited for: 14 -> 16; matrix products, arithmetic and copies ran while one was open for 0% -> 0% of each run, Pallas kernels for 0% -> 0%
where the time goes in v1:
time: 964 us; the launch traced here: 959 us
  waiting for transfers between devices  643 us (67%)
  other arithmetic  240 us (25%)
  local copies, waits for them, and re-layouts  32.2 us (3%)
  between operations  20.8 us (2%)
  matrix products  15.1 us (2%)
    psum x12, waiting for transfers between devices, spread(): return lax.psum(kept, axis)  571 us
    another operation x27, other arithmetic, per_device(): factor = jnp.linalg.cholesky(diag_block)  138 us
    another operation x9, other arithmetic, make_panel(): solved = jax.scipy.linalg.solve_triangular(factor, column.T, lower=True).T  78.8 us
    ppermute x3, waiting for transfers between devices, doubled_up(): theirs = lax.ppermute(grown, axis, [(d, d ^ reach) for d in range(ways)])  56.6 us
  transfers between devices with their start and end apart: 16, of which 16 were waited for; matrix products, arithmetic and copies ran while one was open for 0% of the time, Pallas kernels for 0%

profile of v1, /device:TPU:0, one launch (start us, length us, event | category | flops | bytes accessed | tf_op | source)
XLA Modules:
  0.0 959.2 jit_solution(3199982636884245283)
XLA Ops:
  9.2 2.6 gather_fusion
  11.8 6.3 all-to-all-start
  18.3 15.2 %all-to-all-done = bf16[8,64,440]{2,1,0:T(8,128)(2,1)S(1)} async-done(((bf16[8,64,440]{2,1,0:T(8,128)(2,1)}), bf16[8,64,440]{2,1,0:T(8,128)(2,1)S(1)}, u32[]{:S(2)}, u32[]{:S(2)}) %all-to-all-start) | async-done | bytes 450592 | tf_op jit(solution)/shard_map/all_to_all | solution.py:75
  34.7 1.5 collective-permute-done
  36.5 13.9 %collective-permute-done.1 = bf16[512,440]{1,0:T(8,128)(2,1)S(1)} collective-permute-done((bf16[512,440]{1,0:T(8,128)(2,1)S(1)}, bf16[512,440]{1,0:T(8,128)(2,1)S(1)}, u32[]{:S(2)}, u32[]{:S(2)}) %collective-permute-start.1) | collective-permute-done | bytes 450592 | tf_op jit(solution)/shard_map/ppermute | solution.py:17
  51.7 41.2 %collective-permute-done.2 = bf16[1024,440]{0,1:T(8,128)(2,1)S(1)} collective-permute-done((bf16[1024,440]{0,1:T(8,128)(2,1)S(1)}, bf16[1024,440]{0,1:T(8,128)(2,1)S(1)}, u32[]{:S(2)}, u32[]{:S(2)}) %collective-permute-start.2) | collective-permute-done | bytes 901152 | tf_op jit(solution)/shard_map/ppermute | solution.py:17
  93.4 2.0 maximum_select_fusion
  95.4 2.2 gather_fusion.2
  99.5 41.7 %all-reduce.14.cloned.1.call-done = f32[256,256]{0,1:T(8,128)} async-done(((f32[256,256]{0,1:T(8,128)}), f32[256,256]{0,1:T(8,128)}) %all-reduce.14.cloned.1.call-update) | async-done | bytes 262160 | tf_op jit(solution)/shard_map/psum | solution.py:27
  143.2 11.7 %cholesky.214 = f32[128,128]{1,0:T(8,128)S(1)} custom-call(f32[128,128]{1,0:T(8,128)S(1)} %cholesky.346), custom_call_target="Cholesky" | custom-call | tf_op jit(solution)/shard_map/jit(cholesky)/cholesky | solution.py:108
  155.0 9.8 %custom-call.19 = f32[1,128,128]{1,2,0:T(8,128)S(1)} custom-call(f32[1,128,128]{2,1,0:T(8,128)S(1)} %get-tuple-element.107), custom_call_target="InvertDiagBlocksLowerTriangular" | custom-call | tf_op jit(solution)/shard_map/jit(cholesky)/cholesky | solution.py:108
  165.3 11.7 %cholesky.231 = f32[128,128]{1,0:T(8,128)S(1)} custom-call(f32[128,128]{1,0:T(8,128)S(1)} %convolution_subtract_fusion.8), custom_call_target="Cholesky" | custom-call | tf_op jit(solution)/shard_map/jit(cholesky)/cholesky | solution.py:108
  179.6 4.6 while.8
  184.2 19.7 %custom-call.20 = f32[2,128,128]{1,2,0:T(8,128)S(1)} custom-call(f32[2,128,128]{2,1,0:T(8,128)S(1)} %get-tuple-element.30), custom_call_target="InvertDiagBlocksLowerTriangular" | custom-call | tf_op jit(solution)/shard_map/jit(_solve_triangular)/triangular_solve | solution.py:53
  206.1 56.2 %all-reduce.16.cloned.1.call-done = f32[512,256]{0,1:T(8,128)} async-done(((f32[512,256]{0,1:T(8,128)}), f32[512,256]{0,1:T(8,128)}) %all-reduce.16.cloned.1.call-update) | async-done | bytes 524304 | tf_op jit(solution)/shard_map/psum | solution.py:27
  262.4 1.7 dynamic-slice_select_fusion.3
  264.1 43.7 %all-reduce.18.cloned.1.call-done = f32[256,256]{0,1:T(8,128)} async-done(((f32[256,256]{0,1:T(8,128)}), f32[256,256]{0,1:T(8,128)}) %all-reduce.18.cloned.1.call-update) | async-done | bytes 262160 | tf_op jit(solution)/shard_map/psum | solution.py:27
  307.8 1.8 bitcast_subtract_fusion.2
  310.6 43.7 %all-reduce.20.cloned.1.call-done = f32[256,256]{0,1:T(8,128)} async-done(((f32[256,256]{0,1:T(8,128)}), f32[256,256]{0,1:T(8,128)}) %all-reduce.20.cloned.1.call-update) | async-done | bytes 262160 | tf_op jit(solution)/shard_map/psum | solution.py:27
  356.5 11.7 %cholesky.248 = f32[128,128]{1,0:T(8,128)S(1)} custom-call(f32[128,128]{1,0:T(8,128)S(1)} %cholesky.349), custom_call_target="Cholesky" | custom-call | tf_op jit(solution)/shard_map/jit(cholesky)/cholesky | solution.py:108
  368.2 9.8 %custom-call.21 = f32[1,128,128]{1,2,0:T(8,128)S(1)} custom-call(f32[1,128,128]{2,1,0:T(8,128)S(1)} %get-tuple-element.103), custom_call_target="InvertDiagBlocksLowerTriangular" | custom-call | tf_op jit(solution)/shard_map/jit(cholesky)/cholesky | solution.py:108
  378.5 11.7 %cholesky.265 = f32[128,128]{1,0:T(8,128)S(1)} custom-call(f32[128,128]{1,0:T(8,128)S(1)} %convolution_subtract_fusion.7), custom_call_target="Cholesky" | custom-call | tf_op jit(solution)/shard_map/jit(cholesky)/cholesky | solution.py:108
  393.4 4.3 while.9
  397.7 19.7 %custom-call.22 = f32[2,128,128]{1,2,0:T(8,128)S(1)} custom-call(f32[2,128,128]{2,1,0:T(8,128)S(1)} %get-tuple-element.31), custom_call_target="InvertDiagBlocksLowerTriangular" | custom-call | tf_op jit(solution)/shard_map/jit(_solve_triangular)/triangular_solve | solution.py:53
  419.6 56.3 %all-reduce.22.cloned.1.call-done = f32[512,256]{0,1:T(8,128)} async-done(((f32[512,256]{0,1:T(8,128)}), f32[512,256]{0,1:T(8,128)}) %all-reduce.22.cloned.1.call-update) | async-done | bytes 524304 | tf_op jit(solution)/shard_map/psum | solution.py:27
  475.9 1.7 dynamic-slice_select_fusion.2
  477.6 43.8 %all-reduce.24.cloned.1.call-done = f32[256,256]{0,1:T(8,128)} async-done(((f32[256,256]{0,1:T(8,128)}), f32[256,256]{0,1:T(8,128)}) %all-reduce.24.cloned.1.call-update) | async-done | bytes 262160 | tf_op jit(solution)/shard_map/psum | solution.py:27
  521.4 1.8 bitcast_subtract_fusion.1
  524.1 43.8 %all-reduce.26.cloned.1.call-done = f32[256,256]{0,1:T(8,128)} async-done(((f32[256,256]{0,1:T(8,128)}), f32[256,256]{0,1:T(8,128)}) %all-reduce.26.cloned.1.call-update) | async-done | bytes 262160 | tf_op jit(solution)/shard_map/psum | solution.py:27
  570.0 11.7 %cholesky.282 = f32[128,128]{1,0:T(8,128)S(1)} custom-call(f32[128,128]{1,0:T(8,128)S(1)} %cholesky.352), custom_call_target="Cholesky" | custom-call | tf_op jit(solution)/shard_map/jit(cholesky)/cholesky | solution.py:108
  581.8 9.8 %custom-call.23 = f32[1,128,128]{1,2,0:T(8,128)S(1)} custom-call(f32[1,128,128]{2,1,0:T(8,128)S(1)} %get-tuple-element.99), custom_call_target="InvertDiagBlocksLowerTriangular" | custom-call | tf_op jit(solution)/shard_map/jit(cholesky)/cholesky | solution.py:108
  592.0 11.7 %cholesky.299 = f32[128,128]{1,0:T(8,128)S(1)} custom-call(f32[128,128]{1,0:T(8,128)S(1)} %convolution_subtract_fusion.6), custom_call_target="Cholesky" | custom-call | tf_op jit(solution)/shard_map/jit(cholesky)/cholesky | solution.py:108
  606.9 4.3 while.10
  611.3 19.7 %custom-call.24 = f32[2,128,128]{1,2,0:T(8,128)S(1)} custom-call(f32[2,128,128]{2,1,0:T(8,128)S(1)} %get-tuple-element.32), custom_call_target="InvertDiagBlocksLowerTriangular" | custom-call | tf_op jit(solution)/shard_map/jit(_solve_triangular)/triangular_solve | solution.py:53
  633.1 56.3 %all-reduce.28.cloned.1.call-done = f32[512,256]{0,1:T(8,128)} async-done(((f32[512,256]{0,1:T(8,128)}), f32[512,256]{0,1:T(8,128)}) %all-reduce.28.cloned.1.call-update) | async-done | bytes 524304 | tf_op jit(solution)/shard_map/psum | solution.py:27
  689.4 1.7 dynamic-slice_select_fusion.1
  691.1 43.7 %all-reduce.30.cloned.1.call-done = f32[256,256]{0,1:T(8,128)} async-done(((f32[256,256]{0,1:T(8,128)}), f32[256,256]{0,1:T(8,128)}) %all-reduce.30.cloned.1.call-update) | async-done | bytes 262160 | tf_op jit(solution)/shard_map/psum | solution.py:27
  734.8 1.8 bitcast_subtract_fusion
  737.6 43.8 %all-reduce.32.cloned.1.call-done = f32[256,256]{0,1:T(8,128)} async-done(((f32[256,256]{0,1:T(8,128)}), f32[256,256]{0,1:T(8,128)}) %all-reduce.32.cloned.1.call-update) | async-done | bytes 262160 | tf_op jit(solution)/shard_map/psum | solution.py:27
  783.5 11.7 %cholesky.316 = f32[128,128]{1,0:T(8,128)S(1)} custom-call(f32[128,128]{1,0:T(8,128)S(1)} %cholesky.355), custom_call_target="Cholesky" | custom-call | tf_op jit(solution)/shard_map/jit(cholesky)/cholesky | solution.py:108
  795.3 9.8 %custom-call.25 = f32[1,128,128]{1,2,0:T(8,128)S(1)} custom-call(f32[1,128,128]{2,1,0:T(8,128)S(1)} %get-tuple-element.95), custom_call_target="InvertDiagBlocksLowerTriangular" | custom-call | tf_op jit(solution)/shard_map/jit(cholesky)/cholesky | solution.py:108
  805.6 11.7 %cholesky.333 = f32[128,128]{1,0:T(8,128)S(1)} custom-call(f32[128,128]{1,0:T(8,128)S(1)} %convolution_subtract_fusion.5), custom_call_target="Cholesky" | custom-call | tf_op jit(solution)/shard_map/jit(cholesky)/cholesky | solution.py:108
  820.3 4.2 while.11
  824.5 19.7 %custom-call.26 = f32[2,128,128]{1,2,0:T(8,128)S(1)} custom-call(f32[2,128,128]{2,1,0:T(8,128)S(1)} %get-tuple-element.33), custom_call_target="InvertDiagBlocksLowerTriangular" | custom-call | tf_op jit(solution)/shard_map/jit(_solve_triangular)/triangular_solve | solution.py:53
  847.5 56.3 %all-reduce.34.cloned.1.call-done = f32[512,256]{0,1:T(8,128)} async-done(((f32[512,256]{0,1:T(8,128)}), f32[512,256]{0,1:T(8,128)}) %all-reduce.34.cloned.1.call-update) | async-done | bytes 524304 | tf_op jit(solution)/shard_map/psum | solution.py:27
  903.7 1.7 dynamic-slice_select_fusion
  907.5 41.7 %all-reduce.36.cloned.1.call-done = f32[256,256]{0,1:T(8,128)} async-done(((f32[256,256]{0,1:T(8,128)}), f32[256,256]{0,1:T(8,128)}) %all-reduce.36.cloned.1.call-update) | async-done | bytes 262160 | tf_op jit(solution)/shard_map/psum | solution.py:27
  949.3 1.6 fusion
  (178 shorter events, 56.0 us)
Async XLA Ops:
  9.2 9.0 copy-start.5
  9.2 9.0 copy-start.6
  11.8 21.7 %all-to-all-start = ((bf16[8,64,440]{2,1,0:T(8,128)(2,1)}), bf16[8,64,440]{2,1,0:T(8,128)(2,1)S(1)}, u32[]{:S(2)}, u32[]{:S(2)}) async-start(bf16[8,64,440]{2,1,0:T(8,128)(2,1)} %bitcast.1), calls=%async_computation | async-start | bytes 1048576 | tf_op jit(solution)/shard_map/all_to_all | solution.py:75
  18.1 123.0 %all-reduce.14.cloned.1.call-start = ((), (), s32[]{:S(2)}) async-start(), calls=%async_computation.1 | async-start | bytes 524288 | tf_op jit(solution)/shard_map/psum | solution.py:27
  34.6 1.6 collective-permute-start
  36.4 14.0 %collective-permute-start.1 = (bf16[512,440]{1,0:T(8,128)(2,1)S(1)}, bf16[512,440]{1,0:T(8,128)(2,1)S(1)}, u32[]{:S(2)}, u32[]{:S(2)}) collective-permute-start(bf16[512,440]{1,0:T(8,128)(2,1)S(1)} %maximum_select_fusion.2), channel_id=1, source_target_pairs={{0,2},{1,3},{2,0},{3,1},{4,6},{5,7},{6,4},{7,5},{8,10},{9,11},{10,... | collective-permute-start | bytes 1351688 | tf_op jit(solution)/shard_map/ppermute | solution.py:17
  51.4 41.5 %collective-permute-start.2 = (bf16[1024,440]{0,1:T(8,128)(2,1)S(1)}, bf16[1024,440]{0,1:T(8,128)(2,1)S(1)}, u32[]{:S(2)}, u32[]{:S(2)}) collective-permute-start(bf16[1024,440]{0,1:T(8,128)(2,1)S(1)} %copy.66), channel_id=1, source_target_pairs={{0,4},{1,5},{2,6},{3,7},{4,0},{5,1},{6,2},{7,3},{8,12},{9,13},{10,... | collective-permute-start | bytes 2703368 | tf_op jit(solution)/shard_map/ppermute | solution.py:17
  99.2 163.2 %all-reduce.16.cloned.1.call-start = ((), (), s32[]{:S(2)}) async-start(), calls=%async_computation.2 | async-start | bytes 1048576 | tf_op jit(solution)/shard_map/psum | solution.py:27
  206.1 101.8 %all-reduce.18.cloned.1.call-start = ((), (), s32[]{:S(2)}) async-start(), calls=%async_computation.3 | async-start | bytes 524288 | tf_op jit(solution)/shard_map/psum | solution.py:27
  264.1 90.3 %all-reduce.20.cloned.1.call-start = ((), (), s32[]{:S(2)}) async-start(), calls=%async_computation.4 | async-start | bytes 524288 | tf_op jit(solution)/shard_map/psum | solution.py:27
  310.6 165.3 %all-reduce.22.cloned.1.call-start = ((), (), s32[]{:S(2)}) async-start(), calls=%async_computation.5 | async-start | bytes 1048576 | tf_op jit(solution)/shard_map/psum | solution.py:27
  419.5 101.9 %all-reduce.24.cloned.1.call-start = ((), (), s32[]{:S(2)}) async-start(), calls=%async_computation.6 | async-start | bytes 524288 | tf_op jit(solution)/shard_map/psum | solution.py:27
  477.6 90.3 %all-reduce.26.cloned.1.call-start = ((), (), s32[]{:S(2)}) async-start(), calls=%async_computation.7 | async-start | bytes 524288 | tf_op jit(solution)/shard_map/psum | solution.py:27
  524.0 165.4 %all-reduce.28.cloned.1.call-start = ((), (), s32[]{:S(2)}) async-start(), calls=%async_computation.8 | async-start | bytes 1048576 | tf_op jit(solution)/shard_map/psum | solution.py:27
  633.1 101.8 %all-reduce.30.cloned.1.call-start = ((), (), s32[]{:S(2)}) async-start(), calls=%async_computation.9 | async-start | bytes 524288 | tf_op jit(solution)/shard_map/psum | solution.py:27
  691.1 90.3 %all-reduce.32.cloned.1.call-start = ((), (), s32[]{:S(2)}) async-start(), calls=%async_computation.10 | async-start | bytes 524288 | tf_op jit(solution)/shard_map/psum | solution.py:27
  736.6 107.5 %copy-start.4 = (f32[256,512]{1,0:T(8,128)}, f32[256,512]{1,0:T(8,128)S(1)}, u32[]{:S(2)}) copy-start(f32[256,512]{1,0:T(8,128)S(1)} %get-tuple-element.120) | copy-start | bytes 1572868
  737.5 166.2 %all-reduce.34.cloned.1.call-start = ((), (), s32[]{:S(2)}) async-start(), calls=%async_computation.11 | async-start | bytes 1048576 | tf_op jit(solution)/shard_map/psum | solution.py:27
  844.6 60.9 %copy-start.1 = (f32[512,256]{0,1:T(8,128)S(1)}, f32[512,256]{0,1:T(8,128)}, u32[]{:S(2)}) copy-start(f32[512,256]{0,1:T(8,128)} %all-reduce.16.cloned.1.call-done) | copy-start | bytes 1572868
  844.6 60.9 %copy-start.2 = (f32[512,256]{0,1:T(8,128)S(1)}, f32[512,256]{0,1:T(8,128)}, u32[]{:S(2)}) copy-start(f32[512,256]{0,1:T(8,128)} %all-reduce.22.cloned.1.call-done) | copy-start | bytes 1572868
  844.6 60.9 %copy-start.3 = (f32[512,256]{0,1:T(8,128)S(1)}, f32[512,256]{0,1:T(8,128)}, u32[]{:S(2)}) copy-start(f32[512,256]{0,1:T(8,128)} %all-reduce.28.cloned.1.call-done) | copy-start | bytes 1572868
  847.4 101.9 %all-reduce.36.cloned.1.call-start = ((), (), s32[]{:S(2)}) async-start(), calls=%async_computation.12 | async-start | bytes 524288 | tf_op jit(solution)/shard_map/psum | solution.py:27
  903.7 45.5 %copy-start = (f32[512,256]{0,1:T(8,128)S(1)}, f32[512,256]{0,1:T(8,128)}, u32[]{:S(2)}) copy-start(f32[512,256]{0,1:T(8,128)} %all-reduce.34.cloned.1.call-done) | copy-start | bytes 1572868
Sparse Core Ops, SparseCore 0:
  99.3 41.8 all-reduce.13
  206.2 56.1 all-reduce.15
  265.9 41.8 all-reduce.17
  311.4 42.9 all-reduce.19
  419.7 56.1 all-reduce.21
  479.5 41.8 all-reduce.23
  524.9 42.9 all-reduce.25
  633.2 56.1 all-reduce.27
  692.9 41.8 all-reduce.29
  738.4 42.9 all-reduce.31
  847.5 56.1 all-reduce.33
  907.4 41.8 all-reduce.35
